TPU v7x, 256 devices: a whole 4x4x8 slice. The times are simulated.
256 devices in a mesh: row: 16 (over y_lo, x, core), col: 16 (over y_hi, z).
Axes of the slice: x: 4, y: 4 (y_hi: 2, y_lo: 2; y = y_hi * 2 + y_lo), z: 8, core: 2. Of those that a mesh axis runs over, the one named last changes fastest.
Arguments:
- tiles: bfloat16 [16, 16, 128, 128, 128], P('row', 'col'), as said below
- coords: int32 [16, 16, 2, 128], P('row', 'col'), may hold values from 0 to 63, as said below
- counts: int32 [16, 16], P('row', 'col'), may hold values from 1 to 128, as said below
- valid: int32 [131072], P(('row', 'col')), may hold values 0 or 1
- start: float32 [8, 131072], P(None, ('row', 'col'))
- rotations: float32 [2, 8, 24], replicated, as said below
Outputs:
- eigenmaps: float32 [8, 131072], P(None, ('row', 'col'))
- ritz: float32 [8, 8], replicated
Inputs may be any that keep to these rules, and one draw needn't show every extreme that they name: coords[r, c, 0, s] is a block row from 0 to 63 and coords[r, c, 1, s] a block column from 0 to 63; the live slots of one owner name distinct blocks, each on or above the block diagonal (g_row <= g_col). The live slots of an owner are the first counts[r, c] of its list; one owner in grid row 0 has all 128 live. `tiles`: nonnegative; a tile on the block diagonal is symmetric. The Rayleigh-Ritz coefficients of the current vectors, rotations[t, :, 0 to 7], form a matrix whose diagonal dominates its rows.
All inputs are finite; a program needn't handle non-finite values. No bound on the sum of `valid` on one device may be relied on, other than what follows from the above.
Results may differ from a plain program's by a relative error of at most 0.0013.
Values may be sent and summed in bfloat16 or wider, within the bound.
No kernel may reach another device: no remote copies, remote signals or barrier semaphores. Data moves between devices by JAX's collectives and lax.ppermute only.
A program may use at most 64 MiB of HBM per device.

v0:
```python
import jax
import jax.numpy as jnp
from jax import lax
from jax.sharding import PartitionSpec as P


def matmul_high(left, right):
    return jnp.dot(left, right, precision=lax.Precision.HIGHEST)


def lower_inverse(lower_factor):
    order_size = lower_factor.shape[0]
    identity = jnp.eye(order_size, dtype=lower_factor.dtype)
    inverse_rows = []
    for row_at in range(order_size):
        partial_row = identity[row_at]
        for prior_at in range(row_at):
            partial_row = partial_row - lower_factor[row_at, prior_at] * inverse_rows[prior_at]
        inverse_rows.append(partial_row / lower_factor[row_at, row_at])
    return jnp.stack(inverse_rows)


def settle(new_vecs, new_images, new_steps, step_images, gram_x, gram_ax, node_total):
    lower_factor = jnp.linalg.cholesky(gram_x / node_total)
    inverse = lower_inverse(lower_factor)
    theta = matmul_high(matmul_high(inverse, gram_ax / node_total), inverse.T)
    return (
        matmul_high(inverse, new_vecs),
        matmul_high(inverse, new_images),
        matmul_high(inverse, new_steps),
        matmul_high(inverse, step_images),
        theta,
    )


def gram_sums(new_vecs, new_images):
    return lax.psum(
        (matmul_high(new_vecs, new_vecs.T), matmul_high(new_images, new_vecs.T)), ("row", "col")
    )


def local_terms(
    part_tiles, part_rows, part_cols, weight_direct, weight_mirror, col_blocks, row_blocks
):
    row_span = row_blocks.shape[1]
    col_span = col_blocks.shape[1]
    col_values = jnp.take(col_blocks, part_cols, axis=1)
    row_values = jnp.take(row_blocks, part_rows, axis=1)
    direct = (
        jnp.einsum("sut,cst->csu", part_tiles, col_values, preferred_element_type=jnp.float32)
        * weight_direct[None, :, None]
    )
    mirror = (
        jnp.einsum("sut,csu->cst", part_tiles, row_values, preferred_element_type=jnp.float32)
        * weight_mirror[None, :, None]
    )
    pick_rows = (part_rows[:, None] == jnp.arange(row_span, dtype=jnp.int32)[None, :]).astype(
        jnp.float32
    )
    pick_cols = (part_cols[:, None] == jnp.arange(col_span, dtype=jnp.int32)[None, :]).astype(
        jnp.float32
    )
    rows_sum = jnp.einsum("sp,csu->cpu", pick_rows, direct, precision=lax.Precision.HIGHEST)
    cols_sum = jnp.einsum("sq,cst->cqt", pick_cols, mirror, precision=lax.Precision.HIGHEST)
    return (rows_sum, cols_sum)


def body(tiles, coords, counts, valid, start, rotations):
    row_count = lax.axis_size("row")
    col_count = lax.axis_size("col")
    row_index = lax.axis_index("row")
    col_index = lax.axis_index("col")
    slot_count = tiles.shape[2]
    tile_side = tiles.shape[3]
    stretch_nodes = valid.shape[0]
    per_stretch = stretch_nodes // tile_side
    row_span = col_count * per_stretch
    col_span = row_count * per_stretch
    node_total = jnp.float32(stretch_nodes * row_count * col_count)
    vec_count = start.shape[0]
    flat_tiles = tiles.reshape(slot_count, tile_side, tile_side)
    block_rows = coords[0, 0, 0]
    block_cols = coords[0, 0, 1]
    live_count = counts[0, 0]
    global_rows = row_index * row_span + block_rows
    global_cols = (
        block_cols // per_stretch * col_count + col_index
    ) * per_stretch + block_cols % per_stretch
    live = (jnp.arange(slot_count, dtype=jnp.int32) < live_count).astype(jnp.float32)
    mirror_weight = live * (global_rows != global_cols).astype(jnp.float32)

    def graph_product(vectors):
        width = vectors.shape[0]
        short = vectors.astype(jnp.bfloat16)
        col_side = lax.all_gather(short, "row", axis=1, tiled=True)
        row_side = lax.all_gather(short, "col", axis=1, tiled=True)
        col_blocks = col_side.reshape(width, col_span, tile_side)
        row_blocks = row_side.reshape(width, row_span, tile_side)
        rows_total, cols_total = local_terms(
            flat_tiles, block_rows, block_cols, live, mirror_weight, col_blocks, row_blocks
        )
        direct_part = lax.psum_scatter(
            rows_total.reshape(width, row_span * tile_side), "col", scatter_dimension=1, tiled=True
        )
        mirror_part = lax.psum_scatter(
            cols_total.reshape(width, col_span * tile_side), "row", scatter_dimension=1, tiled=True
        )
        return direct_part + mirror_part

    node_mask = valid.astype(jnp.float32)
    first_vecs = start * node_mask[None, :]
    raw = graph_product(jnp.concatenate([node_mask[None, :], first_vecs], 0))
    degree = raw[0]
    first_images = node_mask[None, :] * (degree[None, :] * first_vecs - raw[1:])
    zero_steps = jnp.zeros_like(first_vecs)
    gram_x, gram_ax = gram_sums(first_vecs, first_images)
    vecs, images, steps, step_images, theta = settle(
        first_vecs, first_images, zero_steps, zero_steps, gram_x, gram_ax, node_total
    )
    for turn in range(rotations.shape[0]):
        resid = images - matmul_high(theta, vecs)
        resid_images = node_mask[None, :] * (degree[None, :] * resid - graph_product(resid))
        stacked = jnp.concatenate([vecs, resid, steps], 0)
        stacked_images = jnp.concatenate([images, resid_images, step_images], 0)
        rotation = rotations[turn]
        new_vecs = matmul_high(rotation, stacked)
        new_images = matmul_high(rotation, stacked_images)
        gram_x, gram_ax = gram_sums(new_vecs, new_images)
        new_steps = matmul_high(rotation[:, vec_count:], stacked[vec_count:])
        new_step_images = matmul_high(rotation[:, vec_count:], stacked_images[vec_count:])
        vecs, images, steps, step_images, theta = settle(
            new_vecs, new_images, new_steps, new_step_images, gram_x, gram_ax, node_total
        )
    return (vecs, theta)


def solution(mesh):
    in_specs = (
        P("row", "col", None, None, None),
        P("row", "col", None, None),
        P("row", "col"),
        P(("row", "col")),
        P(None, ("row", "col")),
        P(),
    )
    out_specs = (P(None, ("row", "col")), P())
    return jax.shard_map(body, mesh=mesh, in_specs=in_specs, out_specs=out_specs, check_vma=False)
```

profile of v0, /device:TPU:1, one launch (start us, length us, event | category | flops | bytes accessed | tf_op | source)
XLA Modules:
  0.0 1272.5 jit_solution(13226586753436208169)
XLA Ops:
  7.2 0.8 compare_and_fusion
  8.0 0.8 slice_bitcast_fusion.2
  8.8 0.7 convert_convert_fusion
  9.5 0.7 multiply_convert_fusion
  10.2 39.4 %all_gather.19 = bf16[9,8192]{1,0:T(8,128)(2,1)S(1)} all-gather(bf16[9,512]{1,0:T(8,128)(2,1)S(1)} %pad_maximum_fusion.8), channel_id=1, replica_groups=mesh['row'=16,'col'=16] {'col'}, dimensions={1}, use_global_device_ids=true | all-gather | bytes 156672 | tf_op jit(solution)/shard_map/all_gather | solution.py:96
  50.5 0.7 gather_fusion.1
  51.2 3.4 fusion.8
  55.3 1.1 copy.34
  56.4 26.8 %all_gather.18 = bf16[9,8192]{1,0:T(8,128)(2,1)S(1)} all-gather(bf16[9,512]{1,0:T(8,128)(2,1)S(1)} %pad_maximum_fusion.8), channel_id=1, replica_groups=mesh['row'=16,'col'=16] {'row'}, dimensions={1}, use_global_device_ids=true | all-gather | bytes 156672 | tf_op jit(solution)/shard_map/all_gather | solution.py:95
  83.4 0.7 gather_fusion
  84.2 4.5 fusion.10
  88.7 0.5 convolution_bitcast_fusion.1
  89.3 1.1 copy.32
  90.7 26.8 %reduce-scatter.9.cloned.1.call-done = f32[9,512]{1,0:T(8,128)} async-done(((f32[9,8192]{1,0:T(8,128)}), f32[9,512]{1,0:T(8,128)}) %reduce-scatter.9.cloned.1.call-update) | async-done | bytes 18448 | tf_op jit(solution)/shard_map/reduce_scatter | solution.py:105
  117.5 198.7 %reduce-scatter.7.cloned.1.call-done = f32[9,512]{1,0:T(8,128)} async-done(((f32[9,8192]{1,0:T(8,128)}), f32[9,512]{1,0:T(8,128)}) %reduce-scatter.7.cloned.1.call-update) | async-done | bytes 18448 | tf_op jit(solution)/shard_map/reduce_scatter | solution.py:102
  316.2 0.8 add.100
  317.1 79.7 %all-reduce.2 = (f32[8,8]{0,1:T(8,128)S(1)}, f32[8,8]{0,1:T(8,128)S(1)}) all-reduce(f32[8,8]{0,1:T(8,128)S(1)} %fusion.95, f32[8,8]{0,1:T(8,128)S(1)} %fusion.87), channel_id=1, replica_groups=mesh['row'=16,'col'=16] {'row','col'}, use_global_device_ids=true, to_apply=%region_0.1 | all-reduce | flops 128 | bytes 1024 | tf_op jit(solution)/shard_map/psum | solution.py:37
  396.9 0.7 cholesky.59
  397.6 0.6 compare_reduce_fusion.2
  398.3 0.6 fusion.110
  398.9 0.7 fusion.147
  399.6 0.7 fusion.148
  400.4 22.6 %subtract_divide_fusion.14 = (f32[1,8]{1,0:T(1,128)S(1)}, f32[1,8]{1,0:T(1,128)S(1)}, f32[1,8]{1,0:T(1,128)S(1)}, f32[1,8]{1,0:T(1,128)S(1)}, f32[1,8]{1,0:T(1,1...) fusion(f32[]{:T(128)} %bitcast.36, f32[]{:T(128)} %bitcast.35, f32[]{:T(128)} %bitcast.34, ...), kind=kLoop, calls=%fused_computation.199 | loop fusion | flops 512 | bytes 656 | tf_op jit(solution)/shard_map/div | solution.py:19
  423.7 31.8 %all_gather.21 = bf16[8,8192]{1,0:T(8,128)(2,1)S(1)} all-gather(bf16[8,512]{1,0:T(8,128)(2,1)S(1)} %get-tuple-element.153), channel_id=1, replica_groups=mesh['row'=16,'col'=16] {'col'}, dimensions={1}, use_global_device_ids=true | all-gather | bytes 139264 | tf_op jit(solution)/shard_map/all_gather | solution.py:96
  455.4 24.9 %all_gather.20 = bf16[8,8192]{1,0:T(8,128)(2,1)S(1)} all-gather(bf16[8,512]{1,0:T(8,128)(2,1)S(1)} %get-tuple-element.153), channel_id=1, replica_groups=mesh['row'=16,'col'=16] {'row'}, dimensions={1}, use_global_device_ids=true | all-gather | bytes 139264 | tf_op jit(solution)/shard_map/all_gather | solution.py:95
  480.4 0.7 gather_fusion.3
  481.1 3.4 fusion.4
  485.0 0.8 copy.69
  485.9 0.7 gather_fusion.2
  486.6 4.5 fusion.6
  491.5 0.9 copy.70
  492.9 0.6 fusion.68
  493.5 45.7 %reduce-scatter.13.cloned.1.call-done = f32[8,512]{1,0:T(8,128)} async-done(((f32[8,8192]{1,0:T(8,128)}), f32[8,512]{1,0:T(8,128)}) %reduce-scatter.13.cloned.1.call-update) | async-done | bytes 16400 | tf_op jit(solution)/shard_map/reduce_scatter | solution.py:105
  539.2 197.1 %reduce-scatter.11.cloned.1.call-done = f32[8,512]{1,0:T(8,128)} async-done(((f32[8,8192]{1,0:T(8,128)}), f32[8,512]{1,0:T(8,128)}) %reduce-scatter.11.cloned.1.call-update) | async-done | bytes 16400 | tf_op jit(solution)/shard_map/reduce_scatter | solution.py:102
  736.3 0.7 subtract_multiply_fusion.1
  737.3 79.8 %all-reduce.1 = (f32[8,8]{0,1:T(8,128)S(1)}, f32[8,8]{0,1:T(8,128)S(1)}) all-reduce(f32[8,8]{0,1:T(8,128)S(1)} %fusion.152, f32[8,8]{0,1:T(8,128)S(1)} %fusion.155), channel_id=1, replica_groups=mesh['row'=16,'col'=16] {'row','col'}, use_global_device_ids=true, to_apply=%region_6.9 | all-reduce | flops 128 | bytes 1024 | tf_op jit(solution)/shard_map/psum | solution.py:37
  817.2 0.7 cholesky.70
  817.9 0.6 compare_reduce_fusion.1
  818.6 0.6 fusion.111
  819.2 0.7 fusion.145
  820.0 0.7 fusion.146
  820.7 22.6 %subtract_divide_fusion.7 = (f32[1,8]{1,0:T(1,128)S(1)}, f32[1,8]{1,0:T(1,128)S(1)}, f32[1,8]{1,0:T(1,128)S(1)}, f32[1,8]{1,0:T(1,128)S(1)}, f32[1,8]{1,0:T(1,12...) fusion(f32[]{:T(128)} %bitcast.87, f32[]{:T(128)} %bitcast.86, f32[]{:T(128)} %bitcast.85, ...), kind=kLoop, calls=%fused_computation.190 | loop fusion | flops 512 | bytes 656 | tf_op jit(solution)/shard_map/div | solution.py:19
  844.0 31.8 %all_gather.23 = bf16[8,8192]{1,0:T(8,128)(2,1)S(1)} all-gather(bf16[8,512]{1,0:T(8,128)(2,1)S(1)} %get-tuple-element.155), channel_id=1, replica_groups=mesh['row'=16,'col'=16] {'col'}, dimensions={1}, use_global_device_ids=true | all-gather | bytes 139264 | tf_op jit(solution)/shard_map/all_gather | solution.py:96
  875.8 24.9 %all_gather.22 = bf16[8,8192]{1,0:T(8,128)(2,1)S(1)} all-gather(bf16[8,512]{1,0:T(8,128)(2,1)S(1)} %get-tuple-element.155), channel_id=1, replica_groups=mesh['row'=16,'col'=16] {'row'}, dimensions={1}, use_global_device_ids=true | all-gather | bytes 139264 | tf_op jit(solution)/shard_map/all_gather | solution.py:95
  900.7 0.7 gather_fusion.5
  901.4 3.4 fusion
  905.3 0.8 copy.67
  906.3 0.7 gather_fusion.4
  906.9 4.5 fusion.2
  911.9 0.9 copy.68
  913.4 0.6 fusion.69
  914.3 45.1 %reduce-scatter.17.cloned.1.call-done = f32[8,512]{1,0:T(8,128)} async-done(((f32[8,8192]{1,0:T(8,128)}), f32[8,512]{1,0:T(8,128)}) %reduce-scatter.17.cloned.1.call-update) | async-done | bytes 16400 | tf_op jit(solution)/shard_map/reduce_scatter | solution.py:105
  959.4 197.2 %reduce-scatter.15.cloned.1.call-done = f32[8,512]{1,0:T(8,128)} async-done(((f32[8,8192]{1,0:T(8,128)}), f32[8,512]{1,0:T(8,128)}) %reduce-scatter.15.cloned.1.call-update) | async-done | bytes 16400 | tf_op jit(solution)/shard_map/reduce_scatter | solution.py:102
  1156.6 0.7 subtract_multiply_fusion
  1157.3 0.6 fusion.62
  1158.2 79.7 %all-reduce = (f32[8,8]{0,1:T(8,128)S(1)}, f32[8,8]{0,1:T(8,128)S(1)}) all-reduce(f32[8,8]{0,1:T(8,128)S(1)} %fusion.158, f32[8,8]{0,1:T(8,128)S(1)} %fusion.161), channel_id=1, replica_groups=mesh['row'=16,'col'=16] {'row','col'}, use_global_device_ids=true, to_apply=%region_10.14 | all-reduce | flops 128 | bytes 1024 | tf_op jit(solution)/shard_map/psum | solution.py:37
  1237.9 0.7 cholesky.81
  1238.7 0.6 compare_reduce_fusion
  1239.3 0.6 select_select_fusion
  1240.0 0.7 fusion.143
  1240.7 0.7 fusion.144
  1241.4 22.6 %subtract_divide_fusion = (f32[1,8]{1,0:T(1,128)S(1)}, f32[1,8]{1,0:T(1,128)S(1)}, f32[1,8]{1,0:T(1,128)S(1)}, f32[1,8]{1,0:T(1,128)S(1)}, f32[1,8]{1,0:T(1,128)...) fusion(f32[]{:T(128)} %bitcast.133, f32[]{:T(128)} %bitcast.132, f32[]{:T(128)} %bitcast.131, ...), kind=kLoop, calls=%fused_computation.183 | loop fusion | flops 512 | bytes 656 | tf_op jit(solution)/shard_map/div | solution.py:19
  1264.0 0.7 fusion.159
  1264.9 0.7 fusion.162
  (77 shorter events, 7.3 us)
Async XLA Ops:
  7.2 47.5 %copy-start.2 = (s32[1,1,2,128]{3,2,1,0:T(2,128)S(1)}, s32[1,1,2,128]{3,2,1,0:T(2,128)}, u32[]{:S(2)}) copy-start(s32[1,1,2,128]{3,2,1,0:T(2,128)} %param.12) | copy-start | bytes 3076
  7.2 110.3 %reduce-scatter.9.cloned.1.call-start = ((), (), s32[]{:S(2)}) async-start(), calls=%async_computation.7 | async-start | bytes 557056 | tf_op jit(solution)/shard_map/reduce_scatter | solution.py:105
  56.4 259.8 %reduce-scatter.7.cloned.1.call-start = ((), (), s32[]{:S(2)}) async-start(), calls=%async_computation.6 | async-start | bytes 557056 | tf_op jit(solution)/shard_map/reduce_scatter | solution.py:102
  84.2 6.3 copy-start.1
  84.2 6.4 copy-start
  90.4 448.7 %reduce-scatter.13.cloned.1.call-start = ((), (), s32[]{:S(2)}) async-start(), calls=%async_computation.9 | async-start | bytes 278528 | tf_op jit(solution)/shard_map/reduce_scatter | solution.py:105
  485.8 250.4 %reduce-scatter.11.cloned.1.call-start = ((), (), s32[]{:S(2)}) async-start(), calls=%async_computation.8 | async-start | bytes 278528 | tf_op jit(solution)/shard_map/reduce_scatter | solution.py:102
  492.5 466.9 %reduce-scatter.17.cloned.1.call-start = ((), (), s32[]{:S(2)}) async-start(), calls=%async_computation.11 | async-start | bytes 278528 | tf_op jit(solution)/shard_map/reduce_scatter | solution.py:105
  906.2 250.4 %reduce-scatter.15.cloned.1.call-start = ((), (), s32[]{:S(2)}) async-start(), calls=%async_computation.10 | async-start | bytes 278528 | tf_op jit(solution)/shard_map/reduce_scatter | solution.py:102
Sparse Core Ops, SparseCore 0:
  56.5 60.9 reduce-scatter.8
  121.8 194.3 reduce-scatter.6
  485.9 53.1 reduce-scatter.12
  543.3 192.9 reduce-scatter.10
  906.3 53.0 reduce-scatter.16
  963.5 193.0 reduce-scatter.14
where the time goes:
time: 1270 us
  waiting for transfers between devices  711 us (56%)
  blocking collectives  419 us (33%)
  other arithmetic  78.4 us (6%)
  matrix products  33.7 us (3%)
  local copies, waits for them, and re-layouts  15.6 us (1%)
  between operations  15.1 us (1%)
    reduce_scatter x3, waiting for transfers between devices, graph_product(): lax.psum_scatter(rows_total.reshape(width, row_span * tile_side), 'col',...  593 us
    psum x3, blocking collectives, gram_sums(): lax.psum((matmul_high(new_vecs, new_vecs.T), matmul_high(new_images, new_...  239 us
    reduce_scatter x3, waiting for transfers between devices, graph_product(): lax.psum_scatter(cols_total.reshape(width, col_span * tile_side), 'row',...  118 us
    all_gather x3, blocking collectives, graph_product(): row_side = lax.all_gather(short, 'col', axis=1, tiled=True)  103 us
    all_gather x3, blocking collectives, graph_product(): col_side = lax.all_gather(short, 'row', axis=1, tiled=True)  76.7 us
    div x3, other arithmetic, lower_inverse(): inverse_rows.append(partial_row / lower_factor[row_at, row_at])  67.8 us
  transfers between devices with their start and end apart: 6, of which 6 were waited for; matrix products, arithmetic and copies ran while one was open for 2% of the time, Pallas kernels for 0%

commit v1 on v0

--- a/solution.py
+++ b/solution.py
@@ -35,7 +35,8 @@
 
 def gram_sums(new_vecs, new_images):
     return lax.psum(
-        (matmul_high(new_vecs, new_vecs.T), matmul_high(new_images, new_vecs.T)), ("row", "col")
+        lax.psum((matmul_high(new_vecs, new_vecs.T), matmul_high(new_images, new_vecs.T)), "col"),
+        "row",
     )
 
 

time: 1270 us -> 1250 us (0.984)
  blocking collectives: 419 us -> 390 us
    psum x3, blocking collectives: 239 us -> 98.1 us  [gram_sums(): lax.psum((matmul_high(new_vecs, new_vecs.T), matmul_high(new_images, new_...]
    psum x0 -> x3, blocking collectives: none -> 120 us  [gram_sums(): lax.psum(lax.psum((matmul_high(new_vecs, new_vecs.T), matmul_high(new_ima...]
where the time goes in v1:
time: 1250 us
  waiting for transfers between devices  714 us (57%)
  blocking collectives  390 us (31%)
  other arithmetic  78.4 us (6%)
  matrix products  33.7 us (3%)
  local copies, waits for them, and re-layouts  15.6 us (1%)
  between operations  15.2 us (1%)
    reduce_scatter x3, waiting for transfers between devices, graph_product(): lax.psum_scatter(rows_total.reshape(width, row_span * tile_side), 'col',...  593 us
    reduce_scatter x3, waiting for transfers between devices, graph_product(): lax.psum_scatter(cols_total.reshape(width, col_span * tile_side), 'row',...  121 us
    psum x3, blocking collectives, gram_sums(): lax.psum(lax.psum((matmul_high(new_vecs, new_vecs.T), matmul_high(new_ima...  120 us
    all_gather x3, blocking collectives, graph_product(): row_side = lax.all_gather(short, 'col', axis=1, tiled=True)  98.2 us
    psum x3, blocking collectives, gram_sums(): lax.psum((matmul_high(new_vecs, new_vecs.T), matmul_high(new_images, new_...  98.1 us
    all_gather x3, blocking collectives, graph_product(): col_side = lax.all_gather(short, 'row', axis=1, tiled=True)  74.3 us
    div x3, other arithmetic, lower_inverse(): inverse_rows.append(partial_row / lower_factor[row_at, row_at])  67.8 us
  transfers between devices with their start and end apart: 6, of which 6 were waited for; matrix products, arithmetic and copies ran while one was open for 2% of the time, Pallas kernels for 0%

profile of v1, /device:TPU:1, one launch (start us, length us, event | category | flops | bytes accessed | tf_op | source)
XLA Modules:
  0.0 1247.0 jit_solution(7502663428791080272)
XLA Ops:
  7.2 0.8 compare_and_fusion
  8.0 0.8 slice_bitcast_fusion.2
  8.8 0.7 convert_convert_fusion
  9.5 0.7 multiply_convert_fusion
  10.2 39.4 %all_gather.19 = bf16[9,8192]{1,0:T(8,128)(2,1)S(1)} all-gather(bf16[9,512]{1,0:T(8,128)(2,1)S(1)} %pad_maximum_fusion.8), channel_id=1, replica_groups=mesh['row'=16,'col'=16] {'col'}, dimensions={1}, use_global_device_ids=true | all-gather | bytes 156672 | tf_op jit(solution)/shard_map/all_gather | solution.py:97
  50.5 0.7 gather_fusion.1
  51.2 3.4 fusion.8
  55.3 1.1 copy.34
  56.4 26.8 %all_gather.18 = bf16[9,8192]{1,0:T(8,128)(2,1)S(1)} all-gather(bf16[9,512]{1,0:T(8,128)(2,1)S(1)} %pad_maximum_fusion.8), channel_id=1, replica_groups=mesh['row'=16,'col'=16] {'row'}, dimensions={1}, use_global_device_ids=true | all-gather | bytes 156672 | tf_op jit(solution)/shard_map/all_gather | solution.py:96
  83.4 0.7 gather_fusion
  84.2 4.5 fusion.10
  89.3 1.1 copy.32
  90.7 26.9 %reduce-scatter.9.cloned.1.call-done = f32[9,512]{1,0:T(8,128)} async-done(((f32[9,8192]{1,0:T(8,128)}), f32[9,512]{1,0:T(8,128)}) %reduce-scatter.9.cloned.1.call-update) | async-done | bytes 18448 | tf_op jit(solution)/shard_map/reduce_scatter | solution.py:106
  117.5 198.7 %reduce-scatter.7.cloned.1.call-done = f32[9,512]{1,0:T(8,128)} async-done(((f32[9,8192]{1,0:T(8,128)}), f32[9,512]{1,0:T(8,128)}) %reduce-scatter.7.cloned.1.call-update) | async-done | bytes 18448 | tf_op jit(solution)/shard_map/reduce_scatter | solution.py:103
  316.2 0.8 add.112
  317.2 32.3 %all-reduce.2 = (f32[8,8]{0,1:T(8,128)S(1)}, f32[8,8]{0,1:T(8,128)S(1)}) all-reduce(f32[8,8]{0,1:T(8,128)S(1)} %fusion.95, f32[8,8]{0,1:T(8,128)S(1)} %fusion.87), channel_id=1, replica_groups=mesh['row'=16,'col'=16] {'col'}, use_global_device_ids=true, to_apply=%region_0.1 | all-reduce | flops 128 | bytes 1024 | tf_op jit(solution)/shard_map/psum | solution.py:38
  349.5 40.2 %all-reduce.5 = (f32[8,8]{0,1:T(8,128)S(1)}, f32[8,8]{0,1:T(8,128)S(1)}) all-reduce(f32[8,8]{0,1:T(8,128)S(1)} %get-tuple-element.9, f32[8,8]{0,1:T(8,128)S(1)} %get-tuple-element.10), channel_id=1, replica_groups=mesh['row'=16,'col'=16] {'row'}, use_global_device_ids=true, to_apply=%region_1.2 | all-reduce | flops 128 | bytes 1024 | tf_op jit(solution)/shard_map/psum | solution.py:37
  389.8 0.7 cholesky.59
  390.5 0.6 compare_reduce_fusion.2
  391.2 0.6 fusion.110
  391.8 0.7 fusion.147
  392.6 0.7 fusion.148
  393.3 22.6 %subtract_divide_fusion.14 = (f32[1,8]{1,0:T(1,128)S(1)}, f32[1,8]{1,0:T(1,128)S(1)}, f32[1,8]{1,0:T(1,128)S(1)}, f32[1,8]{1,0:T(1,128)S(1)}, f32[1,8]{1,0:T(1,1...) fusion(f32[]{:T(128)} %bitcast.36, f32[]{:T(128)} %bitcast.35, f32[]{:T(128)} %bitcast.34, ...), kind=kLoop, calls=%fused_computation.199 | loop fusion | flops 512 | bytes 656 | tf_op jit(solution)/shard_map/div | solution.py:19
  416.6 29.3 %all_gather.21 = bf16[8,8192]{1,0:T(8,128)(2,1)S(1)} all-gather(bf16[8,512]{1,0:T(8,128)(2,1)S(1)} %get-tuple-element.159), channel_id=1, replica_groups=mesh['row'=16,'col'=16] {'col'}, dimensions={1}, use_global_device_ids=true | all-gather | bytes 139264 | tf_op jit(solution)/shard_map/all_gather | solution.py:97
  445.9 23.8 %all_gather.20 = bf16[8,8192]{1,0:T(8,128)(2,1)S(1)} all-gather(bf16[8,512]{1,0:T(8,128)(2,1)S(1)} %get-tuple-element.159), channel_id=1, replica_groups=mesh['row'=16,'col'=16] {'row'}, dimensions={1}, use_global_device_ids=true | all-gather | bytes 139264 | tf_op jit(solution)/shard_map/all_gather | solution.py:96
  469.6 0.7 gather_fusion.3
  470.3 3.4 fusion.4
  474.2 0.8 copy.69
  475.1 0.7 gather_fusion.2
  475.8 4.5 fusion.6
  480.8 0.9 copy.70
  482.1 0.6 fusion.68
  482.8 47.1 %reduce-scatter.13.cloned.1.call-done = f32[8,512]{1,0:T(8,128)} async-done(((f32[8,8192]{1,0:T(8,128)}), f32[8,512]{1,0:T(8,128)}) %reduce-scatter.13.cloned.1.call-update) | async-done | bytes 16400 | tf_op jit(solution)/shard_map/reduce_scatter | solution.py:106
  529.9 197.1 %reduce-scatter.11.cloned.1.call-done = f32[8,512]{1,0:T(8,128)} async-done(((f32[8,8192]{1,0:T(8,128)}), f32[8,512]{1,0:T(8,128)}) %reduce-scatter.11.cloned.1.call-update) | async-done | bytes 16400 | tf_op jit(solution)/shard_map/reduce_scatter | solution.py:103
  727.0 0.7 subtract_multiply_fusion.1
  728.1 32.9 %all-reduce.1 = (f32[8,8]{0,1:T(8,128)S(1)}, f32[8,8]{0,1:T(8,128)S(1)}) all-reduce(f32[8,8]{0,1:T(8,128)S(1)} %fusion.152, f32[8,8]{0,1:T(8,128)S(1)} %fusion.155), channel_id=1, replica_groups=mesh['row'=16,'col'=16] {'col'}, use_global_device_ids=true, to_apply=%region_8.11 | all-reduce | flops 128 | bytes 1024 | tf_op jit(solution)/shard_map/psum | solution.py:38
  761.0 39.7 %all-reduce.4 = (f32[8,8]{0,1:T(8,128)S(1)}, f32[8,8]{0,1:T(8,128)S(1)}) all-reduce(f32[8,8]{0,1:T(8,128)S(1)} %get-tuple-element.7, f32[8,8]{0,1:T(8,128)S(1)} %get-tuple-element.8), channel_id=1, replica_groups=mesh['row'=16,'col'=16] {'row'}, use_global_device_ids=true, to_apply=%region_9.12 | all-reduce | flops 128 | bytes 1024 | tf_op jit(solution)/shard_map/psum | solution.py:37
  800.8 0.7 cholesky.70
  801.6 0.6 compare_reduce_fusion.1
  802.2 0.6 fusion.111
  802.9 0.7 fusion.145
  803.6 0.7 fusion.146
  804.3 22.6 %subtract_divide_fusion.7 = (f32[1,8]{1,0:T(1,128)S(1)}, f32[1,8]{1,0:T(1,128)S(1)}, f32[1,8]{1,0:T(1,128)S(1)}, f32[1,8]{1,0:T(1,128)S(1)}, f32[1,8]{1,0:T(1,12...) fusion(f32[]{:T(128)} %bitcast.87, f32[]{:T(128)} %bitcast.86, f32[]{:T(128)} %bitcast.85, ...), kind=kLoop, calls=%fused_computation.190 | loop fusion | flops 512 | bytes 656 | tf_op jit(solution)/shard_map/div | solution.py:19
  827.6 29.4 %all_gather.23 = bf16[8,8192]{1,0:T(8,128)(2,1)S(1)} all-gather(bf16[8,512]{1,0:T(8,128)(2,1)S(1)} %get-tuple-element.161), channel_id=1, replica_groups=mesh['row'=16,'col'=16] {'col'}, dimensions={1}, use_global_device_ids=true | all-gather | bytes 139264 | tf_op jit(solution)/shard_map/all_gather | solution.py:97
  857.1 23.8 %all_gather.22 = bf16[8,8192]{1,0:T(8,128)(2,1)S(1)} all-gather(bf16[8,512]{1,0:T(8,128)(2,1)S(1)} %get-tuple-element.161), channel_id=1, replica_groups=mesh['row'=16,'col'=16] {'row'}, dimensions={1}, use_global_device_ids=true | all-gather | bytes 139264 | tf_op jit(solution)/shard_map/all_gather | solution.py:96
  880.8 0.7 gather_fusion.5
  881.5 3.4 fusion
  885.4 0.8 copy.67
  886.3 0.7 gather_fusion.4
  887.0 4.5 fusion.2
  892.0 0.9 copy.68
  894.4 46.7 %reduce-scatter.17.cloned.1.call-done = f32[8,512]{1,0:T(8,128)} async-done(((f32[8,8192]{1,0:T(8,128)}), f32[8,512]{1,0:T(8,128)}) %reduce-scatter.17.cloned.1.call-update) | async-done | bytes 16400 | tf_op jit(solution)/shard_map/reduce_scatter | solution.py:106
  941.1 197.0 %reduce-scatter.15.cloned.1.call-done = f32[8,512]{1,0:T(8,128)} async-done(((f32[8,8192]{1,0:T(8,128)}), f32[8,512]{1,0:T(8,128)}) %reduce-scatter.15.cloned.1.call-update) | async-done | bytes 16400 | tf_op jit(solution)/shard_map/reduce_scatter | solution.py:103
  1138.1 0.7 subtract_multiply_fusion
  1139.7 32.9 %all-reduce = (f32[8,8]{0,1:T(8,128)S(1)}, f32[8,8]{0,1:T(8,128)S(1)}) all-reduce(f32[8,8]{0,1:T(8,128)S(1)} %fusion.158, f32[8,8]{0,1:T(8,128)S(1)} %fusion.161), channel_id=1, replica_groups=mesh['row'=16,'col'=16] {'col'}, use_global_device_ids=true, to_apply=%region_14.18 | all-reduce | flops 128 | bytes 1024 | tf_op jit(solution)/shard_map/psum | solution.py:38
  1172.6 39.7 %all-reduce.3 = (f32[8,8]{0,1:T(8,128)S(1)}, f32[8,8]{0,1:T(8,128)S(1)}) all-reduce(f32[8,8]{0,1:T(8,128)S(1)} %get-tuple-element.4, f32[8,8]{0,1:T(8,128)S(1)} %get-tuple-element.6), channel_id=1, replica_groups=mesh['row'=16,'col'=16] {'row'}, use_global_device_ids=true, to_apply=%region_15.19 | all-reduce | flops 128 | bytes 1024 | tf_op jit(solution)/shard_map/psum | solution.py:37
  1212.4 0.7 cholesky.81
  1213.1 0.6 compare_reduce_fusion
  1213.8 0.6 select_select_fusion
  1214.4 0.7 fusion.143
  1215.2 0.7 fusion.144
  1215.9 22.6 %subtract_divide_fusion = (f32[1,8]{1,0:T(1,128)S(1)}, f32[1,8]{1,0:T(1,128)S(1)}, f32[1,8]{1,0:T(1,128)S(1)}, f32[1,8]{1,0:T(1,128)S(1)}, f32[1,8]{1,0:T(1,128)...) fusion(f32[]{:T(128)} %bitcast.133, f32[]{:T(128)} %bitcast.132, f32[]{:T(128)} %bitcast.131, ...), kind=kLoop, calls=%fused_computation.183 | loop fusion | flops 512 | bytes 656 | tf_op jit(solution)/shard_map/div | solution.py:19
  1238.5 0.7 fusion.159
  1239.4 0.7 fusion.162
  (80 shorter events, 9.1 us)
Async XLA Ops:
  7.2 47.5 %copy-start.2 = (s32[1,1,2,128]{3,2,1,0:T(2,128)S(1)}, s32[1,1,2,128]{3,2,1,0:T(2,128)}, u32[]{:S(2)}) copy-start(s32[1,1,2,128]{3,2,1,0:T(2,128)} %param.12) | copy-start | bytes 3076
  7.2 110.4 %reduce-scatter.9.cloned.1.call-start = ((), (), s32[]{:S(2)}) async-start(), calls=%async_computation.7 | async-start | bytes 557056 | tf_op jit(solution)/shard_map/reduce_scatter | solution.py:106
  56.4 259.8 %reduce-scatter.7.cloned.1.call-start = ((), (), s32[]{:S(2)}) async-start(), calls=%async_computation.6 | async-start | bytes 557056 | tf_op jit(solution)/shard_map/reduce_scatter | solution.py:103
  84.1 6.4 copy-start.1
  84.2 6.4 copy-start
  90.4 439.5 %reduce-scatter.13.cloned.1.call-start = ((), (), s32[]{:S(2)}) async-start(), calls=%async_computation.9 | async-start | bytes 278528 | tf_op jit(solution)/shard_map/reduce_scatter | solution.py:106
  475.1 251.9 %reduce-scatter.11.cloned.1.call-start = ((), (), s32[]{:S(2)}) async-start(), calls=%async_computation.8 | async-start | bytes 278528 | tf_op jit(solution)/shard_map/reduce_scatter | solution.py:103
  481.8 459.3 %reduce-scatter.17.cloned.1.call-start = ((), (), s32[]{:S(2)}) async-start(), calls=%async_computation.11 | async-start | bytes 278528 | tf_op jit(solution)/shard_map/reduce_scatter | solution.py:106
  886.3 251.8 %reduce-scatter.15.cloned.1.call-start = ((), (), s32[]{:S(2)}) async-start(), calls=%async_computation.10 | async-start | bytes 278528 | tf_op jit(solution)/shard_map/reduce_scatter | solution.py:103
Sparse Core Ops, SparseCore 0:
  56.5 60.9 reduce-scatter.8
  121.8 194.3 reduce-scatter.6
  475.2 54.6 reduce-scatter.12
  534.0 192.9 reduce-scatter.10
  886.4 54.6 reduce-scatter.16
  945.2 192.7 reduce-scatter.14
